TPU v7x, 256 devices: a whole 4x4x8 slice. The times are simulated.
256 devices in a mesh: dp: 16 (over x, y_hi, core), mp: 16 (over y_lo, z).
Axes of the slice: x: 4, y: 4 (y_hi: 2, y_lo: 2; y = y_hi * 2 + y_lo), z: 8, core: 2. Of those that a mesh axis runs over, the one named last changes fastest.
Arguments:
- tokens: bfloat16 [4096, 4096], P('dp'), may hold values from -32 to 32
- weights: bfloat16 [4096, 2, 3, 4096], P('dp', None, None, 'mp'), may hold values from -1 to 1
- block_modality: int32 [32], replicated, may hold values from 0 to 1
- doc_ids: int32 [4096], replicated, may hold values from 0 to 31, never falling along the last dimension, each value on 1 to 1024 neighbouring positions
- grad_out: bfloat16 [4096, 4096], P('dp', 'mp'), may hold values from -6 to 6
Outputs:
- attended: bfloat16 [4096, 4096], P('dp', 'mp')
- grad_tokens: bfloat16 [4096, 4096], P('dp', 'mp')
- grad_weights: bfloat16 [4096, 2, 3, 4096], P('dp', None, None, 'mp')
Inputs may be any that keep to these rules, and one draw needn't show every extreme that they name: doc_ids never falls along the sequence; a document is a run of equal ids of at most 1024 tokens, and one document has exactly 1024.
All inputs are finite; a program needn't handle non-finite values.
Results may differ from a plain program's by a relative error of at most 0.025.
Values may be sent and summed in bfloat16 or wider, within the bound.
No kernel may reach another device: no remote copies, remote signals or barrier semaphores. Data moves between devices by JAX's collectives and lax.ppermute only.
A program may use at most 128 MiB of HBM per device.

v0:
```python
import jax
import jax.numpy as jnp
from jax import lax
from jax.sharding import PartitionSpec as P

HD = 128
BLOCK = 128
SPAN = 4


def shifted(block, axis, distance):
    devices = range(lax.axis_size(axis))
    route = [(i - distance, i) for i in devices if i - distance in devices]
    return lax.ppermute(block, axis, route)


def split_by_modality(rows, is_image):
    zeros = jnp.zeros_like(rows)
    text = jnp.where(is_image[:, None], zeros, rows)
    image = jnp.where(is_image[:, None], rows, zeros)
    return jnp.stack([text, image], axis=2).reshape(rows.shape[0], 2 * rows.shape[1])


def split_by_modality_major(rows, is_image):
    zeros = jnp.zeros_like(rows)
    text = jnp.where(is_image[:, None], zeros, rows)
    image = jnp.where(is_image[:, None], rows, zeros)
    return jnp.concatenate([text, image], axis=1)


def on_device(tokens, weights, block_modality, doc_ids, grad_out):
    local_rows = tokens.shape[0]
    width_rows = weights.shape[0]
    head_width = weights.shape[3]
    head_count = head_width // HD
    dp_devices = lax.axis_size("dp")
    mp_devices = lax.axis_size("mp")
    local_blocks = local_rows // BLOCK
    front_pad = SPAN * local_rows
    window_len = front_pad + local_rows
    my_index = lax.axis_index("dp")
    scale_factor = HD ** (-0.5)
    token_image = jnp.repeat(block_modality, BLOCK) == 1
    my_image = lax.dynamic_slice_in_dim(token_image, my_index * local_rows, local_rows, 0)
    flat_weights = weights.reshape(width_rows, 2, 3 * head_width)
    whole_weights = lax.all_gather(flat_weights, "dp", axis=0, tiled=True)
    columns = lax.all_to_all(tokens, "dp", split_axis=1, concat_axis=0, tiled=True)
    whole_weights, columns = lax.optimization_barrier((whole_weights, columns))
    stacked_weights = whole_weights.reshape(-1, 3 * head_width)
    summed = jnp.dot(
        split_by_modality(tokens, my_image), stacked_weights, preferred_element_type=jnp.float32
    )
    qkv = summed.astype(jnp.bfloat16).reshape(local_rows, 3, head_count, HD)
    queries = qkv[:, 0]
    key_values = qkv[:, 1:]
    received = []
    for distance in range(SPAN, 0, -1):
        received.append(shifted(key_values, "dp", distance))
    window = jnp.concatenate(received + [key_values], 0)
    key_rows = window[:, 0]
    value_rows = window[:, 1]
    docs_pad = jnp.concatenate([jnp.full((front_pad,), -1, jnp.int32), doc_ids], 0)
    key_docs = lax.dynamic_slice_in_dim(docs_pad, my_index * local_rows, window_len, 0)
    query_docs = lax.dynamic_slice_in_dim(doc_ids, my_index * local_rows, local_rows, 0)
    offsets = jnp.arange(window_len, dtype=jnp.int32) - front_pad
    allowed = (key_docs[None, :] == query_docs[:, None]) & (
        offsets[None, :] <= jnp.arange(local_rows, dtype=jnp.int32)[:, None]
    )
    scores = (
        jnp.einsum("qhd,khd->hqk", queries, key_rows, preferred_element_type=jnp.float32)
        * scale_factor
    )
    scores = jnp.where(allowed[None], scores, -1e30)
    top_score = jnp.max(scores, axis=-1, keepdims=True)
    expos = jnp.where(allowed[None], jnp.exp(scores - top_score), 0.0)
    probs_f = expos / jnp.sum(expos, axis=-1, keepdims=True)
    probs = probs_f.astype(jnp.bfloat16)
    attended = jnp.einsum("hqk,khd->qhd", probs, value_rows, preferred_element_type=jnp.float32)
    attended = attended.astype(jnp.bfloat16).reshape(local_rows, head_width)
    upstream = grad_out.reshape(local_rows, head_count, HD)
    dprob = jnp.einsum("qhd,khd->hqk", upstream, value_rows, preferred_element_type=jnp.float32)
    row_delta = jnp.sum(probs_f * dprob, axis=-1, keepdims=True)
    dscore = (probs_f * (dprob - row_delta)).astype(jnp.bfloat16)
    grad_q = (
        jnp.einsum("hqk,khd->qhd", dscore, key_rows, preferred_element_type=jnp.float32)
        * scale_factor
    )
    grad_k = (
        jnp.einsum("hqk,qhd->khd", dscore, queries, preferred_element_type=jnp.float32)
        * scale_factor
    )
    grad_v = jnp.einsum("hqk,qhd->khd", probs, upstream, preferred_element_type=jnp.float32)
    window_grads = jnp.stack([grad_k, grad_v], 1)
    own_grads = window_grads[front_pad:]
    for distance in range(1, SPAN + 1):
        lower_edge = front_pad - distance * local_rows
        sent_block = window_grads[lower_edge : lower_edge + local_rows]
        own_grads = own_grads + shifted(sent_block.astype(jnp.bfloat16), "dp", -distance).astype(
            sent_block.dtype
        )
    dqkv = (
        jnp.concatenate([grad_q[:, None], own_grads], 1)
        .astype(jnp.bfloat16)
        .reshape(local_rows, 3 * head_width)
    )
    parts = lax.dot_general(
        split_by_modality_major(dqkv, my_image),
        whole_weights.reshape(whole_weights.shape[0], -1),
        (((1,), (1,)), ((), ())),
        preferred_element_type=jnp.float32,
    ).astype(jnp.bfloat16)
    group_parts = lax.all_to_all(
        parts.reshape(local_rows, mp_devices, -1), "mp", split_axis=1, concat_axis=1, tiled=True
    )
    grad_tokens = jnp.sum(group_parts.astype(jnp.float32), axis=1).astype(jnp.bfloat16)
    gathered = lax.all_gather(dqkv, "dp", axis=0, tiled=True)
    weight_sum = lax.dot_general(
        columns,
        split_by_modality_major(gathered, token_image),
        (((0,), (0,)), ((), ())),
        preferred_element_type=jnp.float32,
    )
    grad_weights = weight_sum.astype(jnp.bfloat16).reshape(width_rows, 2, 3, head_width)
    return (attended, grad_tokens, grad_weights)


def solution(mesh):
    return jax.shard_map(
        on_device,
        mesh=mesh,
        in_specs=(P("dp", None), P("dp", None, None, "mp"), P(), P(), P("dp", "mp")),
        out_specs=(P("dp", "mp"), P("dp", "mp"), P("dp", None, None, "mp")),
        check_vma=False,
    )
```

profile of v0, /device:TPU:33, one launch (start us, length us, event | category | flops | bytes accessed | tf_op | source)
XLA Modules:
  0.0 316.9 jit_solution(15968421403756851934)
XLA Ops:
  7.2 3.2 copy.46
  10.4 2.5 copy.47
  12.9 7.7 %all-to-all-start = ((bf16[256,16,256]{0,2,1:T(8,128)(2,1)}), bf16[256,16,256]{0,2,1:T(8,128)(2,1)}, u32[]{:S(2)}, u32[]{:S(2)}) async-start(bf16[256,16,256]{0,2,1:T(8,128)(2,1)} %bitcast.76), calls=%async_computation | async-start | bytes 4194304 | tf_op jit(solution)/shard_map/all_to_all | solution.py:47
  21.0 2.3 select_bitcast_fusion.1
  23.3 33.3 %all-to-all-done = bf16[256,16,256]{0,2,1:T(8,128)(2,1)} async-done(((bf16[256,16,256]{0,2,1:T(8,128)(2,1)}), bf16[256,16,256]{0,2,1:T(8,128)(2,1)}, u32[]{:S(2)}, u32[]{:S(2)}) %all-to-all-start) | async-done | bytes 2097184 | tf_op jit(solution)/shard_map/all_to_all | solution.py:47
  56.6 4.1 %copy.48 = bf16[16,256,256]{2,1,0:T(8,128)(2,1)} copy(bf16[16,256,256]{1,2,0:T(8,128)(2,1)} %bitcast.5) | data formatting | bytes 4194304 | tf_op jit(solution)/shard_map/all_to_all | solution.py:47
  60.7 75.9 %all-gather.3.cloned.1.call-done = bf16[4096,2,768]{0,2,1:T(8,128)(2,1)} async-done(((bf16[256,2,768]{0,2,1:T(8,128)(2,1)}), bf16[4096,2,768]{0,2,1:T(8,128)(2,1)}) %all-gather.3.cloned.1.call-update) | async-done | bytes 12582928 | tf_op jit(solution)/shard_map/all_gather | solution.py:46
  136.6 8.6 %fusion.22 = bf16[256,768]{1,0:T(8,128)(2,1)S(1)} fusion(bf16[4096,2,768]{0,2,1:T(8,128)(2,1)} %all-gather.3.cloned.1.call-done, bf16[256,4096,1]{1,0,2:T(8,128)(2,1)} %get-tuple-element.22, bf16[256,4096,1]{1,0,2:T(8,128)(2,1)S(1)} %copy-done.2), kind=kOutput, calls=%fused_computation.35 | convolution fusion | flops 3223519232 | bytes 17170432 | tf_op jit(solution)/shard_map/dot_general | solution.py:50
  145.6 2.8 collective-permute-start
  150.5 2.1 collective-permute-start.2
  153.0 5.0 %collective-permute-start.3 = (bf16[256,2,2,128]{3,0,2,1:T(8,128)(2,1)S(1)}, bf16[256,2,2,128]{3,0,2,1:T(8,128)(2,1)S(1)}, u32[]{:S(2)}, u32[]{:S(2)}) collective-permute-start(bf16[256,2,2,128]{3,0,2,1:T(8,128)(2,1)S(1)} %copy.67), channel_id=1, source_target_pairs={{0,16},{16,32},{32,48},{48,64},{64,80},{80,96},{96,112},{112,128},... | collective-permute-start | bytes 786440 | tf_op jit(solution)/shard_map/ppermute | solution.py:14
  160.4 2.4 collective-permute-done.3
  164.4 2.5 fusion.45
  166.9 2.2 multiply_reduce_fusion
  174.6 2.1 collective-permute-start.4
  178.3 3.4 %collective-permute-done.7 = bf16[256,2,2,128]{0,3,2,1:T(8,128)(2,1)S(1)} collective-permute-done((bf16[256,2,2,128]{0,3,2,1:T(8,128)(2,1)S(1)}, bf16[256,2,2,128]{0,3,2,1:T(8,128)(2,1)S(1)}, u32[]{:S(2)}, u32[]{:S(2)}) %collective-permute-start.7) | collective-permute-done | bytes 262176 | tf_op jit(solution)/shard_map/ppermute | solution.py:14
  181.7 10.9 %collective-permute-done.6 = bf16[256,2,2,128]{0,3,2,1:T(8,128)(2,1)S(1)} collective-permute-done((bf16[256,2,2,128]{0,3,2,1:T(8,128)(2,1)S(1)}, bf16[256,2,2,128]{0,3,2,1:T(8,128)(2,1)S(1)}, u32[]{:S(2)}, u32[]{:S(2)}) %collective-permute-start.6) | collective-permute-done | bytes 262176 | tf_op jit(solution)/shard_map/ppermute | solution.py:14
  194.7 8.3 %convolution_convert_fusion = bf16[256,4096]{1,0:T(8,128)(2,1)S(1)} fusion(bf16[4096,1536]{0,1:T(8,128)(2,1)} %bitcast.74, bf16[256,768]{0,1:T(8,128)(2,1)S(1)} %get-tuple-element.28, bf16[256,768]{0,1:T(8,128)(2,1)S(1)} %get-tuple-element.27), kind=kOutput, calls=%fused_computation.7 | convolution fusion | flops 3223846912 | bytes 15466496 | tf_op jit(solution)/shard_map/dot_general | solution.py:106
  204.6 7.9 %all-to-all-start.1 = ((bf16[256,16,256]{2,0,1:T(8,128)(2,1)}), bf16[256,16,256]{2,0,1:T(8,128)(2,1)S(1)}, u32[]{:S(2)}, u32[]{:S(2)}) async-start(bf16[256,16,256]{2,0,1:T(8,128)(2,1)} %bitcast.77), calls=%async_computation.1 | async-start | bytes 4194304 | tf_op jit(solution)/shard_map/all_to_all | solution.py:112
  212.5 2.7 convolution_convert_fusion.1
  216.0 42.3 %all-to-all-done.1 = bf16[256,16,256]{2,0,1:T(8,128)(2,1)S(1)} async-done(((bf16[256,16,256]{2,0,1:T(8,128)(2,1)}), bf16[256,16,256]{2,0,1:T(8,128)(2,1)S(1)}, u32[]{:S(2)}, u32[]{:S(2)}) %all-to-all-start.1) | async-done | bytes 2097184 | tf_op jit(solution)/shard_map/all_to_all | solution.py:112
  259.2 31.4 %all-gather.5.cloned.1.call-done = bf16[4096,768]{0,1:T(8,128)(2,1)} async-done(((bf16[256,768]{0,1:T(8,128)(2,1)}), bf16[4096,768]{0,1:T(8,128)(2,1)}) %all-gather.5.cloned.1.call-update) | async-done | bytes 6291472 | tf_op jit(solution)/shard_map/all_gather | solution.py:116
  290.7 6.3 %broadcast_select_fusion.1 = (bf16[4096,768]{0,1:T(8,128)(2,1)S(1)}, bf16[4096,768]{0,1:T(8,128)(2,1)}) fusion(bf16[4096,768]{0,1:T(8,128)(2,1)} %all-gather.5.cloned.1.call-done, pred[4096]{0:T(1024)(128)(4,1)S(1)} %broadcast_bitcast_fusion), kind=kLoop, calls=%fused_computation.6 | loop fusion | flops 6291456 | bytes 18878464 | tf_op jit(solution)/shard_map/jit(_where)/select_n | solution.py:26
  297.0 9.9 %fusion.15 = bf16[256,1536]{1,0:T(8,128)(2,1)} fusion(bf16[4096,256]{1,0:T(8,128)(2,1)} %bitcast.81, bf16[4096,768]{0,1:T(8,128)(2,1)} %get-tuple-element.20, bf16[4096,768]{0,1:T(8,128)(2,1)S(1)} %get-tuple-element.19), kind=kOutput, calls=%fused_computation.27 | convolution fusion | flops 3246784512 | bytes 15466496 | tf_op jit(solution)/shard_map/dot_general | solution.py:117
  (55 shorter events, 22.6 us)
Async XLA Ops:
  7.2 3.2 %copy-start = (bf16[256,4096]{1,0:T(8,128)(2,1)S(1)}, bf16[256,4096]{1,0:T(8,128)(2,1)}, u32[]{:S(2)}) copy-start(bf16[256,4096]{1,0:T(8,128)(2,1)} %param.5) | copy-start | bytes 6291460
  7.2 129.4 %all-gather.3.cloned.1.call-start = ((), (), s32[]{:S(2)}) async-start(), calls=%async_computation.2 | async-start | bytes 13369344 | tf_op jit(solution)/shard_map/all_gather | solution.py:46
  12.9 7.8 %copy-start.5 = (s32[32]{0:T(128)S(1)}, s32[32]{0:T(128)}, u32[]{:S(2)}) copy-start(s32[32]{0:T(128)} %param.7) | copy-start | bytes 388
  12.9 8.0 %copy-start.4 = (s32[4096]{0:T(1024)S(1)}, s32[4096]{0:T(1024)}, u32[]{:S(2)}) copy-start(s32[4096]{0:T(1024)} %param.8) | copy-start | bytes 49156
  12.9 43.7 %all-to-all-start = ((bf16[256,16,256]{0,2,1:T(8,128)(2,1)}), bf16[256,16,256]{0,2,1:T(8,128)(2,1)}, u32[]{:S(2)}, u32[]{:S(2)}) async-start(bf16[256,16,256]{0,2,1:T(8,128)(2,1)} %bitcast.76), calls=%async_computation | async-start | bytes 4194304 | tf_op jit(solution)/shard_map/all_to_all | solution.py:47
  20.6 270.1 %all-gather.5.cloned.1.call-start = ((), (), s32[]{:S(2)}) async-start(), calls=%async_computation.3 | async-start | bytes 6684672 | tf_op jit(solution)/shard_map/all_gather | solution.py:116
  56.6 80.0 %copy-start.2 = (bf16[256,4096,1]{1,0,2:T(8,128)(2,1)S(1)}, bf16[256,4096,1]{1,0,2:T(8,128)(2,1)}, u32[]{:S(2)}) copy-start(bf16[256,4096,1]{1,0,2:T(8,128)(2,1)} %get-tuple-element.21) | copy-start | bytes 6291460
  145.2 7.7 %copy-start.3 = (bf16[256,256]{1,0:T(8,128)(2,1)S(1)}, bf16[256,256]{1,0:T(8,128)(2,1)}, u32[]{:S(2)}) copy-start(bf16[256,256]{1,0:T(8,128)(2,1)} %param.9) | copy-start | bytes 393220
  145.6 12.6 %collective-permute-start = (bf16[256,2,2,128]{3,0,2,1:T(8,128)(2,1)S(1)}, bf16[256,2,2,128]{3,0,2,1:T(8,128)(2,1)S(1)}, u32[]{:S(2)}, u32[]{:S(2)}) collective-permute-start(bf16[256,2,2,128]{3,0,2,1:T(8,128)(2,1)S(1)} %copy.67), channel_id=1, source_target_pairs={{0,64},{16,80},{32,96},{48,112},{64,128},{80,144},{96,160},{112,17... | collective-permute-start | bytes 786440 | tf_op jit(solution)/shard_map/ppermute | solution.py:14
  148.4 10.5 %collective-permute-start.1 = (bf16[256,2,2,128]{3,0,2,1:T(8,128)(2,1)S(1)}, bf16[256,2,2,128]{3,0,2,1:T(8,128)(2,1)S(1)}, u32[]{:S(2)}, u32[]{:S(2)}) collective-permute-start(bf16[256,2,2,128]{3,0,2,1:T(8,128)(2,1)S(1)} %copy.67), channel_id=1, source_target_pairs={{0,48},{16,64},{32,80},{48,96},{64,112},{80,128},{96,144},{112,160... | collective-permute-start | bytes 786440 | tf_op jit(solution)/shard_map/ppermute | solution.py:14
  150.5 9.2 %collective-permute-start.2 = (bf16[256,2,2,128]{3,0,2,1:T(8,128)(2,1)S(1)}, bf16[256,2,2,128]{3,0,2,1:T(8,128)(2,1)S(1)}, u32[]{:S(2)}, u32[]{:S(2)}) collective-permute-start(bf16[256,2,2,128]{3,0,2,1:T(8,128)(2,1)S(1)} %copy.67), channel_id=1, source_target_pairs={{0,32},{16,48},{32,64},{48,80},{64,96},{80,112},{96,128},{112,144}... | collective-permute-start | bytes 786440 | tf_op jit(solution)/shard_map/ppermute | solution.py:14
  153.0 9.8 %collective-permute-start.3 = (bf16[256,2,2,128]{3,0,2,1:T(8,128)(2,1)S(1)}, bf16[256,2,2,128]{3,0,2,1:T(8,128)(2,1)S(1)}, u32[]{:S(2)}, u32[]{:S(2)}) collective-permute-start(bf16[256,2,2,128]{3,0,2,1:T(8,128)(2,1)S(1)} %copy.67), channel_id=1, source_target_pairs={{0,16},{16,32},{32,48},{48,64},{64,80},{80,96},{96,112},{112,128},... | collective-permute-start | bytes 786440 | tf_op jit(solution)/shard_map/ppermute | solution.py:14
  166.9 2.6 copy-start.1
  170.7 11.1 %collective-permute-start.7 = (bf16[256,2,2,128]{0,3,2,1:T(8,128)(2,1)S(1)}, bf16[256,2,2,128]{0,3,2,1:T(8,128)(2,1)S(1)}, u32[]{:S(2)}, u32[]{:S(2)}) collective-permute-start(bf16[256,2,2,128]{0,3,2,1:T(8,128)(2,1)S(1)} %get-tuple-element.24), channel_id=1, source_target_pairs={{64,0},{80,16},{96,32},{112,48},{128,64},{144,80},{160,96},{176,11... | collective-permute-start | bytes 786440 | tf_op jit(solution)/shard_map/ppermute | solution.py:14
  172.0 20.7 %collective-permute-start.6 = (bf16[256,2,2,128]{0,3,2,1:T(8,128)(2,1)S(1)}, bf16[256,2,2,128]{0,3,2,1:T(8,128)(2,1)S(1)}, u32[]{:S(2)}, u32[]{:S(2)}) collective-permute-start(bf16[256,2,2,128]{0,3,2,1:T(8,128)(2,1)S(1)} %get-tuple-element.25), channel_id=1, source_target_pairs={{48,0},{64,16},{80,32},{96,48},{112,64},{128,80},{144,96},{160,112... | collective-permute-start | bytes 786440 | tf_op jit(solution)/shard_map/ppermute | solution.py:14
  173.3 19.4 %collective-permute-start.5 = (bf16[256,2,2,128]{0,3,2,1:T(8,128)(2,1)S(1)}, bf16[256,2,2,128]{0,3,2,1:T(8,128)(2,1)S(1)}, u32[]{:S(2)}, u32[]{:S(2)}) collective-permute-start(bf16[256,2,2,128]{0,3,2,1:T(8,128)(2,1)S(1)} %get-tuple-element.26), channel_id=1, source_target_pairs={{32,0},{48,16},{64,32},{80,48},{96,64},{112,80},{128,96},{144,112}... | collective-permute-start | bytes 786440 | tf_op jit(solution)/shard_map/ppermute | solution.py:14
  174.6 18.1 %collective-permute-start.4 = (bf16[256,2,2,128]{0,3,2,1:T(8,128)(2,1)S(1)}, bf16[256,2,2,128]{0,3,2,1:T(8,128)(2,1)S(1)}, u32[]{:S(2)}, u32[]{:S(2)}) collective-permute-start(bf16[256,2,2,128]{0,3,2,1:T(8,128)(2,1)S(1)} %get-tuple-element.23), channel_id=1, source_target_pairs={{16,0},{32,16},{48,32},{64,48},{80,64},{96,80},{112,96},{128,112},... | collective-permute-start | bytes 786440 | tf_op jit(solution)/shard_map/ppermute | solution.py:14
  204.6 53.7 %all-to-all-start.1 = ((bf16[256,16,256]{2,0,1:T(8,128)(2,1)}), bf16[256,16,256]{2,0,1:T(8,128)(2,1)S(1)}, u32[]{:S(2)}, u32[]{:S(2)}) async-start(bf16[256,16,256]{2,0,1:T(8,128)(2,1)} %bitcast.77), calls=%async_computation.1 | async-start | bytes 4194304 | tf_op jit(solution)/shard_map/all_to_all | solution.py:112
Sparse Core Ops, SparseCore 0:
  11.1 125.4 all-gather.2
  193.8 96.8 all-gather.4
where the time goes:
time: 318 us; the launch traced here: 317 us
  waiting for transfers between devices  200 us (63%)
  matrix products  36.8 us (12%)
  starting transfers between devices  33.7 us (11%)
  local copies, waits for them, and re-layouts  19.8 us (6%)
  between operations  14.3 us (4%)
  other arithmetic  12.6 us (4%)
    all_gather x1, waiting for transfers between devices, on_device(): whole_weights = lax.all_gather(flat_weights, 'dp', axis=0, tiled=True)  75.9 us
    all_to_all x1, waiting for transfers between devices, on_device(): lax.all_to_all(parts.reshape(local_rows, mp_devices, -1), 'mp', split_axi...  42.3 us
    all_to_all x1, waiting for transfers between devices, on_device(): lax.all_to_all(tokens, 'dp', split_axis=1, concat_axis=0, tiled=True)  33.3 us
    all_gather x1, waiting for transfers between devices, on_device(): gathered = lax.all_gather(dqkv, 'dp', axis=0, tiled=True)  31.4 us
    ppermute x8, starting transfers between devices, shifted(): return lax.ppermute(block, axis, route)  18 us
    ppermute x8, waiting for transfers between devices, shifted(): return lax.ppermute(block, axis, route)  16.8 us
    unnamed x21, local copies, waits for them, and re-layouts  11.2 us
    dot_general x1, matrix products, on_device(): lax.dot_general(columns, split_by_modality_major(gathered, token_image),...  9.91 us
  transfers between devices with their start and end apart: 12, of which 7 were waited for; matrix products, arithmetic and copies ran while one was open for 9% of the time, Pallas kernels for 0%

commit v1 on v0

--- a/solution.py
+++ b/solution.py
@@ -43,7 +43,9 @@
     token_image = jnp.repeat(block_modality, BLOCK) == 1
     my_image = lax.dynamic_slice_in_dim(token_image, my_index * local_rows, local_rows, 0)
     flat_weights = weights.reshape(width_rows, 2, 3 * head_width)
-    whole_weights = lax.all_gather(flat_weights, "dp", axis=0, tiled=True)
+    whole_weights = jnp.concatenate(
+        lax.all_to_all(jnp.stack([flat_weights] * lax.axis_size("dp")), "dp", 0, 0), axis=0
+    )
     columns = lax.all_to_all(tokens, "dp", split_axis=1, concat_axis=0, tiled=True)
     whole_weights, columns = lax.optimization_barrier((whole_weights, columns))
     stacked_weights = whole_weights.reshape(-1, 3 * head_width)

time: 318 us -> 460 us (1.45)
  waiting for transfers between devices: 200 us -> 312 us
  local copies, waits for them, and re-layouts: 19.8 us -> 39.1 us
  starting transfers between devices: 33.7 us -> 44.6 us
    all_to_all x0 -> x1, waiting for transfers between devices: none -> 194 us  [on_device(): lax.all_to_all(jnp.stack([flat_weights] * lax.axis_size('dp')), 'dp', 0, 0)]
    all_gather x1 -> x0, waiting for transfers between devices: 75.9 us -> none  [on_device(): whole_weights = lax.all_gather(flat_weights, 'dp', axis=0, tiled=True)]
    reshape x0 -> x1, local copies, waits for them, and re-layouts: none -> 11.4 us  [on_device(): jnp.concatenate(lax.all_to_all(jnp.stack([flat_weights] * lax.axis_size('...]
    all_to_all x1, waiting for transfers between devices: 33.3 us -> 26.2 us  [on_device(): lax.all_to_all(tokens, 'dp', split_axis=1, concat_axis=0, tiled=True)]
    ppermute x8, waiting for transfers between devices: 16.8 us -> 10.2 us  [shifted(): return lax.ppermute(block, axis, route)]
    another operation x0 -> x1, local copies, waits for them, and re-layouts: none -> 5.96 us  [on_device(): jnp.stack([flat_weights] * lax.axis_size('dp'))]
    all_to_all x0 -> x1, starting transfers between devices: none -> 5.8 us  [on_device(): lax.all_to_all(jnp.stack([flat_weights] * lax.axis_size('dp')), 'dp', 0, 0)]
    all_gather x1, waiting for transfers between devices: 31.4 us -> 37.1 us  [on_device(): gathered = lax.all_gather(dqkv, 'dp', axis=0, tiled=True)]
  transfers between devices with their start and end apart: 12 -> 12, of which waited for: 7 -> 7; matrix products, arithmetic and copies ran while one was open for 9% -> 6% of each run, Pallas kernels for 0% -> 0%
where the time goes in v1:
time: 460 us; the launch traced here: 458 us
  waiting for transfers between devices  312 us (68%)
  starting transfers between devices  44.6 us (10%)
  local copies, waits for them, and re-layouts  39.1 us (8%)
  matrix products  36 us (8%)
  between operations  14.3 us (3%)
  other arithmetic  12.7 us (3%)
    all_to_all x1, waiting for transfers between devices, on_device(): lax.all_to_all(jnp.stack([flat_weights] * lax.axis_size('dp')), 'dp', 0, 0)  194 us
    all_to_all x1, waiting for transfers between devices, on_device(): lax.all_to_all(parts.reshape(local_rows, mp_devices, -1), 'mp', split_axi...  44.7 us
    all_gather x1, waiting for transfers between devices, on_device(): gathered = lax.all_gather(dqkv, 'dp', axis=0, tiled=True)  37.1 us
    all_to_all x1, waiting for transfers between devices, on_device(): lax.all_to_all(tokens, 'dp', split_axis=1, concat_axis=0, tiled=True)  26.2 us
    ppermute x8, starting transfers between devices, shifted(): return lax.ppermute(block, axis, route)  23 us
    unnamed x25, local copies, waits for them, and re-layouts  13.3 us
    reshape x1, local copies, waits for them, and re-layouts, on_device(): jnp.concatenate(lax.all_to_all(jnp.stack([flat_weights] * lax.axis_size('...  11.4 us
    ppermute x8, waiting for transfers between devices, shifted(): return lax.ppermute(block, axis, route)  10.2 us
  transfers between devices with their start and end apart: 12, of which 7 were waited for; matrix products, arithmetic and copies ran while one was open for 6% of the time, Pallas kernels for 0%

profile of v1, /device:TPU:33, one launch (start us, length us, event | category | flops | bytes accessed | tf_op | source)
XLA Modules:
  0.0 458.5 jit_solution(4023950677850059465)
XLA Ops:
  7.2 4.1 copy.48
  11.3 7.6 %all-to-all-start.1 = ((bf16[256,16,256]{0,2,1:T(8,128)(2,1)}), bf16[256,16,256]{0,2,1:T(8,128)(2,1)S(1)}, u32[]{:S(2)}, u32[]{:S(2)}) async-start(bf16[256,16,256]{0,2,1:T(8,128)(2,1)} %bitcast.81), calls=%async_computation.1 | async-start | bytes 4194304 | tf_op jit(solution)/shard_map/all_to_all | solution.py:49
  18.9 2.2 copy.46
  21.1 26.2 %all-to-all-done.1 = bf16[256,16,256]{0,2,1:T(8,128)(2,1)S(1)} async-done(((bf16[256,16,256]{0,2,1:T(8,128)(2,1)}), bf16[256,16,256]{0,2,1:T(8,128)(2,1)S(1)}, u32[]{:S(2)}, u32[]{:S(2)}) %all-to-all-start.1) | async-done | bytes 2097184 | tf_op jit(solution)/shard_map/all_to_all | solution.py:49
  48.6 6.0 %stack.24 = bf16[16,256,2,768]{1,3,2,0:T(8,128)(2,1)} broadcast(bf16[256,2,768]{0,2,1:T(8,128)(2,1)S(1)} %bitcast.83), dimensions={1,2,3} | broadcast | bytes 13369344 | tf_op jit(solution)/shard_map/stack | solution.py:47
  54.6 5.8 %all-to-all-start = ((bf16[16,256,2,768]{1,3,2,0:T(8,128)(2,1)}), bf16[16,256,2,768]{1,3,2,0:T(8,128)(2,1)}, u32[]{:S(2)}, u32[]{:S(2)}) async-start(bf16[16,256,2,768]{1,3,2,0:T(8,128)(2,1)} %stack.24), calls=%async_computation | async-start | bytes 25165824 | tf_op jit(solution)/shard_map/all_to_all | solution.py:47
  60.8 2.4 select_bitcast_fusion.1
  63.2 3.9 copy.49
  67.1 193.6 %all-to-all-done = bf16[16,256,2,768]{1,3,2,0:T(8,128)(2,1)} async-done(((bf16[16,256,2,768]{1,3,2,0:T(8,128)(2,1)}), bf16[16,256,2,768]{1,3,2,0:T(8,128)(2,1)}, u32[]{:S(2)}, u32[]{:S(2)}) %all-to-all-start) | async-done | bytes 12582944 | tf_op jit(solution)/shard_map/all_to_all | solution.py:47
  260.7 11.4 %copy.72 = bf16[16,2,96,8,256]{4,3,0,2,1:T(8,128)(2,1)} copy(bf16[16,2,96,8,256]{4,3,2,1,0:T(8,128)(2,1)} %bitcast.30) | data formatting | bytes 25165824 | tf_op jit(solution)/shard_map/reshape | solution.py:46
  272.1 8.0 %fusion.22 = bf16[256,768]{1,0:T(8,128)(2,1)S(1)} fusion(bf16[4096,2,768]{0,2,1:T(8,128)(2,1)} %bitcast.76, bf16[256,4096,1]{1,0,2:T(8,128)(2,1)S(1)} %copy-done.4, bf16[256,4096,1]{1,0,2:T(8,128)(2,1)S(1)} %copy-done.3), kind=kOutput, calls=%fused_computation.35 | convolution fusion | flops 3223519232 | bytes 17170432 | tf_op jit(solution)/shard_map/dot_general | solution.py:52
  283.1 9.9 %collective-permute-start.2 = (bf16[256,2,2,128]{3,0,2,1:T(8,128)(2,1)S(1)}, bf16[256,2,2,128]{3,0,2,1:T(8,128)(2,1)S(1)}, u32[]{:S(2)}, u32[]{:S(2)}) collective-permute-start(bf16[256,2,2,128]{3,0,2,1:T(8,128)(2,1)S(1)} %copy.68), channel_id=1, source_target_pairs={{0,32},{16,48},{32,64},{48,80},{64,96},{80,112},{96,128},{112,144}... | collective-permute-start | bytes 786440 | tf_op jit(solution)/shard_map/ppermute | solution.py:14
  293.4 4.5 collective-permute-start.3
  302.8 2.5 fusion.45
  305.3 2.2 multiply_reduce_fusion
  313.0 2.1 collective-permute-start.4
  316.8 8.5 %collective-permute-done.6 = bf16[256,2,2,128]{0,3,2,1:T(8,128)(2,1)S(1)} collective-permute-done((bf16[256,2,2,128]{0,3,2,1:T(8,128)(2,1)S(1)}, bf16[256,2,2,128]{0,3,2,1:T(8,128)(2,1)S(1)}, u32[]{:S(2)}, u32[]{:S(2)}) %collective-permute-start.6) | collective-permute-done | bytes 262176 | tf_op jit(solution)/shard_map/ppermute | solution.py:14
  328.0 8.3 %convolution_convert_fusion = bf16[256,4096]{1,0:T(8,128)(2,1)S(1)} fusion(bf16[4096,1536]{0,1:T(8,128)(2,1)} %bitcast.77, bf16[256,768]{0,1:T(8,128)(2,1)S(1)} %get-tuple-element.28, bf16[256,768]{0,1:T(8,128)(2,1)S(1)} %get-tuple-element.27), kind=kOutput, calls=%fused_computation.7 | convolution fusion | flops 3223846912 | bytes 15466496 | tf_op jit(solution)/shard_map/dot_general | solution.py:108
  337.9 8.1 %all-to-all-start.2 = ((bf16[256,16,256]{2,0,1:T(8,128)(2,1)}), bf16[256,16,256]{2,0,1:T(8,128)(2,1)S(1)}, u32[]{:S(2)}, u32[]{:S(2)}) async-start(bf16[256,16,256]{2,0,1:T(8,128)(2,1)} %bitcast.80), calls=%async_computation.2 | async-start | bytes 4194304 | tf_op jit(solution)/shard_map/all_to_all | solution.py:114
  346.1 2.6 convolution_convert_fusion.1
  349.4 44.7 %all-to-all-done.2 = bf16[256,16,256]{2,0,1:T(8,128)(2,1)S(1)} async-done(((bf16[256,16,256]{2,0,1:T(8,128)(2,1)}), bf16[256,16,256]{2,0,1:T(8,128)(2,1)S(1)}, u32[]{:S(2)}, u32[]{:S(2)}) %all-to-all-start.2) | async-done | bytes 2097184 | tf_op jit(solution)/shard_map/all_to_all | solution.py:114
  395.1 37.1 %all-gather.2.cloned.1.call-done = bf16[4096,768]{0,1:T(8,128)(2,1)} async-done(((bf16[256,768]{0,1:T(8,128)(2,1)}), bf16[4096,768]{0,1:T(8,128)(2,1)}) %all-gather.2.cloned.1.call-update) | async-done | bytes 6291472 | tf_op jit(solution)/shard_map/all_gather | solution.py:118
  432.2 6.3 %broadcast_select_fusion.1 = (bf16[4096,768]{0,1:T(8,128)(2,1)S(1)}, bf16[4096,768]{0,1:T(8,128)(2,1)}) fusion(bf16[4096,768]{0,1:T(8,128)(2,1)} %all-gather.2.cloned.1.call-done, pred[4096]{0:T(1024)(128)(4,1)S(1)} %broadcast_bitcast_fusion), kind=kLoop, calls=%fused_computation.6 | loop fusion | flops 6291456 | bytes 18878464 | tf_op jit(solution)/shard_map/jit(_where)/select_n | solution.py:26
  438.5 9.9 %fusion.15 = bf16[256,1536]{1,0:T(8,128)(2,1)} fusion(bf16[4096,256]{1,0:T(8,128)(2,1)} %bitcast.85, bf16[4096,768]{0,1:T(8,128)(2,1)} %get-tuple-element.20, bf16[4096,768]{0,1:T(8,128)(2,1)S(1)} %get-tuple-element.19), kind=kOutput, calls=%fused_computation.27 | convolution fusion | flops 3246784512 | bytes 15466496 | tf_op jit(solution)/shard_map/dot_general | solution.py:119
  (60 shorter events, 26.2 us)
Async XLA Ops:
  11.3 36.1 %all-to-all-start.1 = ((bf16[256,16,256]{0,2,1:T(8,128)(2,1)}), bf16[256,16,256]{0,2,1:T(8,128)(2,1)S(1)}, u32[]{:S(2)}, u32[]{:S(2)}) async-start(bf16[256,16,256]{0,2,1:T(8,128)(2,1)} %bitcast.81), calls=%async_computation.1 | async-start | bytes 4194304 | tf_op jit(solution)/shard_map/all_to_all | solution.py:49
  47.3 1.3 copy-start.1
  54.6 5.9 %copy-start.7 = (s32[32]{0:T(128)S(1)}, s32[32]{0:T(128)}, u32[]{:S(2)}) copy-start(s32[32]{0:T(128)} %param.7) | copy-start | bytes 388
  54.6 6.0 %copy-start.6 = (s32[4096]{0:T(1024)S(1)}, s32[4096]{0:T(1024)}, u32[]{:S(2)}) copy-start(s32[4096]{0:T(1024)} %param.8) | copy-start | bytes 49156
  54.6 6.2 %copy-start = (bf16[256,4096]{1,0:T(8,128)(2,1)S(1)}, bf16[256,4096]{1,0:T(8,128)(2,1)}, u32[]{:S(2)}) copy-start(bf16[256,4096]{1,0:T(8,128)(2,1)} %param.5) | copy-start | bytes 6291460
  54.6 206.1 %all-to-all-start = ((bf16[16,256,2,768]{1,3,2,0:T(8,128)(2,1)}), bf16[16,256,2,768]{1,3,2,0:T(8,128)(2,1)}, u32[]{:S(2)}, u32[]{:S(2)}) async-start(bf16[16,256,2,768]{1,3,2,0:T(8,128)(2,1)} %stack.24), calls=%async_computation | async-start | bytes 25165824 | tf_op jit(solution)/shard_map/all_to_all | solution.py:47
  60.4 371.8 %all-gather.2.cloned.1.call-start = ((), (), s32[]{:S(2)}) async-start(), calls=%async_computation.3 | async-start | bytes 6684672 | tf_op jit(solution)/shard_map/all_gather | solution.py:118
  260.7 11.4 %copy-start.3 = (bf16[256,4096,1]{1,0,2:T(8,128)(2,1)S(1)}, bf16[256,4096,1]{1,0,2:T(8,128)(2,1)}, u32[]{:S(2)}) copy-start(bf16[256,4096,1]{1,0,2:T(8,128)(2,1)} %get-tuple-element.21) | copy-start | bytes 6291460
  260.7 11.4 %copy-start.4 = (bf16[256,4096,1]{1,0,2:T(8,128)(2,1)S(1)}, bf16[256,4096,1]{1,0,2:T(8,128)(2,1)}, u32[]{:S(2)}) copy-start(bf16[256,4096,1]{1,0,2:T(8,128)(2,1)} %get-tuple-element.22) | copy-start | bytes 6291460
  280.1 13.2 %copy-start.5 = (bf16[256,256]{1,0:T(8,128)(2,1)S(1)}, bf16[256,256]{1,0:T(8,128)(2,1)}, u32[]{:S(2)}) copy-start(bf16[256,256]{1,0:T(8,128)(2,1)} %param.9) | copy-start | bytes 393220
  280.5 17.6 %collective-permute-start = (bf16[256,2,2,128]{3,0,2,1:T(8,128)(2,1)S(1)}, bf16[256,2,2,128]{3,0,2,1:T(8,128)(2,1)S(1)}, u32[]{:S(2)}, u32[]{:S(2)}) collective-permute-start(bf16[256,2,2,128]{3,0,2,1:T(8,128)(2,1)S(1)} %copy.68), channel_id=1, source_target_pairs={{0,64},{16,80},{32,96},{48,112},{64,128},{80,144},{96,160},{112,17... | collective-permute-start | bytes 786440 | tf_op jit(solution)/shard_map/ppermute | solution.py:14
  281.8 17.0 %collective-permute-start.1 = (bf16[256,2,2,128]{3,0,2,1:T(8,128)(2,1)S(1)}, bf16[256,2,2,128]{3,0,2,1:T(8,128)(2,1)S(1)}, u32[]{:S(2)}, u32[]{:S(2)}) collective-permute-start(bf16[256,2,2,128]{3,0,2,1:T(8,128)(2,1)S(1)} %copy.68), channel_id=1, source_target_pairs={{0,48},{16,64},{32,80},{48,96},{64,112},{80,128},{96,144},{112,160... | collective-permute-start | bytes 786440 | tf_op jit(solution)/shard_map/ppermute | solution.py:14
  283.1 16.5 %collective-permute-start.2 = (bf16[256,2,2,128]{3,0,2,1:T(8,128)(2,1)S(1)}, bf16[256,2,2,128]{3,0,2,1:T(8,128)(2,1)S(1)}, u32[]{:S(2)}, u32[]{:S(2)}) collective-permute-start(bf16[256,2,2,128]{3,0,2,1:T(8,128)(2,1)S(1)} %copy.68), channel_id=1, source_target_pairs={{0,32},{16,48},{32,64},{48,80},{64,96},{80,112},{96,128},{112,144}... | collective-permute-start | bytes 786440 | tf_op jit(solution)/shard_map/ppermute | solution.py:14
  293.4 7.8 %collective-permute-start.3 = (bf16[256,2,2,128]{3,0,2,1:T(8,128)(2,1)S(1)}, bf16[256,2,2,128]{3,0,2,1:T(8,128)(2,1)S(1)}, u32[]{:S(2)}, u32[]{:S(2)}) collective-permute-start(bf16[256,2,2,128]{3,0,2,1:T(8,128)(2,1)S(1)} %copy.68), channel_id=1, source_target_pairs={{0,16},{16,32},{32,48},{48,64},{64,80},{80,96},{96,112},{112,128},... | collective-permute-start | bytes 786440 | tf_op jit(solution)/shard_map/ppermute | solution.py:14
  305.3 2.6 copy-start.2
  309.1 7.7 %collective-permute-start.7 = (bf16[256,2,2,128]{0,3,2,1:T(8,128)(2,1)S(1)}, bf16[256,2,2,128]{0,3,2,1:T(8,128)(2,1)S(1)}, u32[]{:S(2)}, u32[]{:S(2)}) collective-permute-start(bf16[256,2,2,128]{0,3,2,1:T(8,128)(2,1)S(1)} %get-tuple-element.24), channel_id=1, source_target_pairs={{64,0},{80,16},{96,32},{112,48},{128,64},{144,80},{160,96},{176,11... | collective-permute-start | bytes 786440 | tf_op jit(solution)/shard_map/ppermute | solution.py:14
  310.4 14.9 %collective-permute-start.6 = (bf16[256,2,2,128]{0,3,2,1:T(8,128)(2,1)S(1)}, bf16[256,2,2,128]{0,3,2,1:T(8,128)(2,1)S(1)}, u32[]{:S(2)}, u32[]{:S(2)}) collective-permute-start(bf16[256,2,2,128]{0,3,2,1:T(8,128)(2,1)S(1)} %get-tuple-element.25), channel_id=1, source_target_pairs={{48,0},{64,16},{80,32},{96,48},{112,64},{128,80},{144,96},{160,112... | collective-permute-start | bytes 786440 | tf_op jit(solution)/shard_map/ppermute | solution.py:14
  311.7 13.6 %collective-permute-start.5 = (bf16[256,2,2,128]{0,3,2,1:T(8,128)(2,1)S(1)}, bf16[256,2,2,128]{0,3,2,1:T(8,128)(2,1)S(1)}, u32[]{:S(2)}, u32[]{:S(2)}) collective-permute-start(bf16[256,2,2,128]{0,3,2,1:T(8,128)(2,1)S(1)} %get-tuple-element.26), channel_id=1, source_target_pairs={{32,0},{48,16},{64,32},{80,48},{96,64},{112,80},{128,96},{144,112}... | collective-permute-start | bytes 786440 | tf_op jit(solution)/shard_map/ppermute | solution.py:14
  313.0 13.0 %collective-permute-start.4 = (bf16[256,2,2,128]{0,3,2,1:T(8,128)(2,1)S(1)}, bf16[256,2,2,128]{0,3,2,1:T(8,128)(2,1)S(1)}, u32[]{:S(2)}, u32[]{:S(2)}) collective-permute-start(bf16[256,2,2,128]{0,3,2,1:T(8,128)(2,1)S(1)} %get-tuple-element.23), channel_id=1, source_target_pairs={{16,0},{32,16},{48,32},{64,48},{80,64},{96,80},{112,96},{128,112},... | collective-permute-start | bytes 786440 | tf_op jit(solution)/shard_map/ppermute | solution.py:14
  337.9 56.2 %all-to-all-start.2 = ((bf16[256,16,256]{2,0,1:T(8,128)(2,1)}), bf16[256,16,256]{2,0,1:T(8,128)(2,1)S(1)}, u32[]{:S(2)}, u32[]{:S(2)}) async-start(bf16[256,16,256]{2,0,1:T(8,128)(2,1)} %bitcast.80), calls=%async_computation.2 | async-start | bytes 4194304 | tf_op jit(solution)/shard_map/all_to_all | solution.py:114
Sparse Core Ops, SparseCore 0:
  327.1 105.0 all-gather.1
